TPU v7x, 128 devices: a whole 4x4x4 slice. The times are simulated.
128 devices in a mesh: group: 8 (over y, core), member: 16 (over z, x).
Axes of the slice: x: 4, y: 4, z: 4, core: 2. Of those that a mesh axis runs over, the one named last changes fastest.
Arguments:
- candidates: bfloat16 [512, 64, 1024], P('member', 'group'), may hold values from -6 to 6
- kv_cache: bfloat16 [64, 2048, 2048], P('group', 'member'), may hold values from -6 to 6
- cache_request: int32 [64], replicated, may hold values from 0 to 63, as said below
- rank_request: int32 [64], replicated, may hold values from 0 to 63, as said below
- hist_blocks: int32 [64], replicated, may hold values from 1 to 16, 544 in all
- w_uq: bfloat16 [1024, 2048], replicated, may hold values from -0.1875 to 0.1875
- w_out: bfloat16 [1024, 1024], replicated, may hold values from -0.1875 to 0.1875
Outputs:
- ranked: bfloat16 [512, 64, 1024], P('member', 'group')
Inputs may be any that keep to these rules, and one draw needn't show every extreme that they name: `cache_request`: A permutation; cache row q lies on group q // 8, events split over member. `rank_request`: A permutation; group g ranks positions g * 8 to (g + 1) * 8 - 1. The requests cached on one group are dealt out to the ranking groups in turn, so every pair of groups carries 8 // 8 or 1 requests and some pair carries exactly 1; the uneven part of the load is the live history lengths.
All inputs are finite; a program needn't handle non-finite values.
Results may differ from a plain program's by a relative error of at most 0.011.
Values may be sent and summed in bfloat16 or wider, within the bound.
No kernel may reach another device: no remote copies, remote signals or barrier semaphores. Data moves between devices by JAX's collectives and lax.ppermute only.
A program may use at most 320 MiB of HBM per device.

v0:
```python
import jax
import jax.numpy as jnp
from jax import lax
from jax.sharding import PartitionSpec as P

HEADS = 8
BLK = 128


def layer_norm(values):
    center = values - jnp.mean(values, axis=-1, keepdims=True)
    spread = jnp.mean(center * center, axis=-1, keepdims=True)
    return center * lax.rsqrt(spread + 1e-05)


def routing(cache_request, rank_request, per_group):
    slot_ids = jnp.arange(cache_request.shape[0], dtype=jnp.int32)
    match = cache_request[:, None] == rank_request[None, :]
    rank_pos = jnp.sum(jnp.where(match, slot_ids[None, :], 0), axis=1)
    target = rank_pos // per_group
    owner_grp = slot_ids // per_group
    earlier = (
        (owner_grp[:, None] == owner_grp[None, :])
        & (target[:, None] == target[None, :])
        & (slot_ids[None, :] < slot_ids[:, None])
    )
    arrival = jnp.sum(earlier.astype(jnp.int32), axis=1)
    slot_of_pos = jnp.sum(jnp.where(match, slot_ids[:, None], 0), axis=0)
    return (target, arrival, slot_of_pos)


def attend(piece, queries, live, scale):
    width = queries.shape[2] * queries.shape[3]
    count = piece.shape[1]
    keys = piece[:, :, :width].reshape(piece.shape[0], count, queries.shape[2], queries.shape[3])
    values = piece[:, :, width:].reshape(piece.shape[0], count, queries.shape[2], queries.shape[3])
    scores = jnp.einsum("crhd,rehd->rhce", queries, keys, preferred_element_type=jnp.float32)
    events = jnp.arange(count).astype(jnp.float32)
    keep = (events[None, :] < live[:, None]).astype(jnp.float32) / live[:, None]
    weights = (jax.nn.silu(scores * scale) * keep[:, None, None, :]).astype(jnp.bfloat16)
    return jnp.einsum("rhce,rehd->crhd", weights, values, preferred_element_type=jnp.float32)


def on_device(candidates, kv_cache, cache_request, rank_request, hist_blocks, w_uq, w_out):
    groups = lax.axis_size("group")
    per_group = kv_cache.shape[0]
    cand_rows = candidates.shape[0]
    width = candidates.shape[2]
    head_dim = width // HEADS
    capacity = (per_group + groups - 1) // groups
    group_now = lax.axis_index("group")
    target, arrival, slot_of_pos = routing(cache_request, rank_request, per_group)
    first_slot = group_now * per_group
    local_target = lax.dynamic_slice_in_dim(target, first_slot, per_group)
    local_arrival = lax.dynamic_slice_in_dim(arrival, first_slot, per_group)
    target_grid = jnp.arange(groups)[:, None, None]
    place_grid = jnp.arange(capacity)[None, :, None]
    hits = (local_target[None, None, :] == target_grid) & (
        local_arrival[None, None, :] == place_grid
    )
    chosen = jnp.sum(jnp.where(hits, jnp.arange(per_group)[None, None, :], 0), axis=2).reshape(-1)
    filled = jnp.any(hits, axis=2).reshape(-1)
    positions = first_slot + jnp.arange(per_group)
    source_slot = slot_of_pos[positions]
    receive_index = source_slot // per_group * capacity + arrival[source_slot]
    live = (hist_blocks[rank_request[positions]] * BLK).astype(jnp.float32)
    inputs = candidates.astype(jnp.float32)
    normed = layer_norm(inputs).astype(jnp.bfloat16).reshape(cand_rows * per_group, width)
    projected = jax.nn.silu(jnp.dot(normed, w_uq, preferred_element_type=jnp.float32))
    gates = projected[:, :width].reshape(cand_rows, per_group, width)
    queries = (
        projected[:, width:].astype(jnp.bfloat16).reshape(cand_rows, per_group, HEADS, head_dim)
    )
    scale = head_dim ** (-0.5)
    outgoing = jnp.where(filled[:, None, None], kv_cache[chosen], jnp.zeros((), jnp.bfloat16))
    incoming = lax.all_to_all(outgoing, "group", split_axis=0, concat_axis=0, tiled=True)
    panels = incoming[receive_index]
    attn = attend(lax.all_gather(panels, "member", axis=1, tiled=True), queries, live, scale)
    attn = attn.reshape(cand_rows, per_group, width)
    gated = (layer_norm(attn) * gates).astype(jnp.bfloat16).reshape(cand_rows * per_group, width)
    result = jnp.dot(gated, w_out, preferred_element_type=jnp.float32) + inputs.reshape(
        cand_rows * per_group, width
    )
    return result.astype(jnp.bfloat16).reshape(cand_rows, per_group, width)


def solution(mesh):
    return jax.shard_map(
        on_device,
        mesh=mesh,
        in_specs=(P("member", "group", None), P("group", "member", None), P(), P(), P(), P(), P()),
        out_specs=P("member", "group", None),
        check_vma=False,
    )
```

profile of v0, /device:TPU:1, one launch (start us, length us, event | category | flops | bytes accessed | tf_op | source)
XLA Modules:
  0.0 615.8 jit_solution(919087667570539489)
XLA Ops:
  6.5 1.0 fusion.26
  7.6 0.2 convert_reduce_fusion.1
  7.9 0.1 select_reduce_fusion
  8.2 5.0 gather_fusion
  13.1 4.5 broadcast_select_fusion
  17.6 6.0 all-to-all-start
  23.6 0.6 gather_fusion.1
  24.3 0.6 gather_fusion.2
  25.0 47.4 %all-to-all-done = bf16[8,128,2048]{2,1,0:T(8,128)(2,1)} async-done(((bf16[8,128,2048]{2,1,0:T(8,128)(2,1)}), bf16[8,128,2048]{2,1,0:T(8,128)(2,1)}, u32[]{:S(2)}, u32[]{:S(2)}) %all-to-all-start) | async-done | bytes 4194336 | tf_op jit(solution)/shard_map/all_to_all | solution.py:76
  72.4 5.0 gather_fusion.3
  77.4 0.6 copy-done.1
  78.0 0.6 gather_fusion.4
  78.7 0.6 gather_fusion.5
  79.3 0.1 convert_reduce_fusion
  79.5 0.3 fusion.8
  79.8 3.7 divide_multiply_fusion
  83.5 1.3 copy-done.4
  85.0 361.7 %all-gather.3.cloned.1.call-done = bf16[8,2048,2048]{2,1,0:T(8,128)(2,1)} async-done(((bf16[8,128,2048]{2,1,0:T(8,128)(2,1)}), bf16[8,2048,2048]{2,1,0:T(8,128)(2,1)}) %all-gather.3.cloned.1.call-update) | async-done | bytes 67108880 | tf_op jit(solution)/shard_map/all_gather | solution.py:78
  446.7 43.3 %fusion.37 = (bf16[8,2048,1024]{2,1,0:T(8,128)(2,1)}, bf16[8,2048,1024]{2,1,0:T(8,128)(2,1)}) fusion(bf16[8,2048,2048]{2,1,0:T(8,128)(2,1)} %all-gather.3.cloned.1.call-done), kind=kLoop, calls=%fused_computation.86 | loop fusion | bytes 134217728 | tf_op jit(solution)/shard_map/slice | solution.py:35
  490.0 42.2 %copy.44 = bf16[8,2048,1024]{1,2,0:T(8,128)(2,1)} copy(bf16[8,2048,1024]{2,1,0:T(8,128)(2,1)} %get-tuple-element.7) | data formatting | bytes 67108864 | tf_op jit(solution)/shard_map/slice | solution.py:35
  532.3 42.2 %copy.43 = bf16[8,2048,1024]{1,2,0:T(8,128)(2,1)} copy(bf16[8,2048,1024]{2,1,0:T(8,128)(2,1)} %get-tuple-element.8) | data formatting | bytes 67108864 | tf_op jit(solution)/shard_map/slice | solution.py:36
  574.5 29.0 %fusion.38 = (f32[32,8]{0,1:T(8,128)S(1)}, f32[32,8,8,128]{3,0,2,1:T(8,128)}) fusion(bf16[8,2048,8,128]{1,3,2,0:T(8,128)(2,1)} %bitcast.58, f32[8,2048]{1,0:T(8,128)S(1)} %convert_divide_fusion, bf16[8,2048,8,128]{1,3,2,0:T(8,128)(2,1)} %bitcast.57, bf16[32,8,8,128]{3,1,2,0:T(8,128)(2,1)S(1)} %fusion.12), kind=kOutput, calls=%fused_computation.87 | convolution fusion | flops 2177105664 | bytes 68748288 | tf_op jit(solution)/shard_map/rhce,rehd->crhd/dot_general | solution.py:41
  603.7 1.5 multiply_reduce_fusion
  605.4 3.5 fusion.7
  (37 shorter events, 1.0 us)
Async XLA Ops:
  6.5 598.9 %copy-start = (bf16[1024,1024]{1,0:T(8,128)(2,1)S(1)}, bf16[1024,1024]{1,0:T(8,128)(2,1)}, u32[]{:S(2)}) copy-start(bf16[1024,1024]{1,0:T(8,128)(2,1)} %param.13) | copy-start | bytes 6291460
  17.6 54.7 %all-to-all-start = ((bf16[8,128,2048]{2,1,0:T(8,128)(2,1)}), bf16[8,128,2048]{2,1,0:T(8,128)(2,1)}, u32[]{:S(2)}, u32[]{:S(2)}) async-start(bf16[8,128,2048]{2,1,0:T(8,128)(2,1)} %broadcast_select_fusion), calls=%async_computation | async-start | bytes 8388608 | tf_op jit(solution)/shard_map/all_to_all | solution.py:76
  23.6 423.1 %all-gather.3.cloned.1.call-start = ((), (), s32[]{:S(2)}) async-start(), calls=%async_computation.1 | async-start | bytes 71303168 | tf_op jit(solution)/shard_map/all_gather | solution.py:78
  77.4 0.7 copy-start.1
  77.4 1.3 copy-start.2
  77.4 2.0 copy-start.3
  83.5 1.4 copy-start.4
Sparse Core Ops, SparseCore 0:
  77.5 369.1 all-gather.2
where the time goes:
time: 618 us; the launch traced here: 616 us
  waiting for transfers between devices  409 us (66%)
  local copies, waits for them, and re-layouts  143 us (23%)
  matrix products  36.2 us (6%)
  between operations  13.5 us (2%)
  other arithmetic  8.11 us (1%)
    all_gather x1, waiting for transfers between devices, on_device(): lax.all_gather(panels, 'member', axis=1, tiled=True)  362 us
    slice x2, local copies, waits for them, and re-layouts, attend(): piece[:, :, :width]  85.6 us
    all_to_all x1, waiting for transfers between devices, on_device(): lax.all_to_all(outgoing, 'group', split_axis=0, concat_axis=0, tiled=True)  47.4 us
    slice x1, local copies, waits for them, and re-layouts, attend(): piece[:, :, width:]  42.2 us
    dot_general x1, matrix products, attend(): jnp.einsum('rhce,rehd->crhd', weights, values, preferred_element_type=jnp...  29 us
  transfers between devices with their start and end apart: 2, of which 2 were waited for; matrix products, arithmetic and copies ran while one was open for 1% of the time, Pallas kernels for 0%

commit v1 on v0

--- a/solution.py
+++ b/solution.py
@@ -5,6 +5,17 @@
 
 HEADS = 8
 BLK = 128
+
+
+def cut_along(x, dim, size):
+    before, after = (x.shape[:dim], x.shape[dim + 1 :])
+    return jnp.moveaxis(x.reshape(*before, size, -1, *after), dim, 0)
+
+
+def joined_along(blocks, dim):
+    blocks = jnp.moveaxis(blocks, 0, dim)
+    shape = blocks.shape
+    return blocks.reshape(*shape[:dim], shape[dim] * shape[dim + 1], *shape[dim + 2 :])
 
 
 def layer_norm(values):
@@ -73,7 +84,14 @@
     )
     scale = head_dim ** (-0.5)
     outgoing = jnp.where(filled[:, None, None], kv_cache[chosen], jnp.zeros((), jnp.bfloat16))
-    incoming = lax.all_to_all(outgoing, "group", split_axis=0, concat_axis=0, tiled=True)
+    size, position = (lax.axis_size("group"), lax.axis_index("group"))
+    tiles = cut_along(outgoing, 0, size)
+    outs = [tiles[position]]
+    for step in range(1, size):
+        sent = tiles[position ^ step]
+        outs.append(lax.ppermute(sent, "group", [(i, i ^ step) for i in range(size)]))
+    tiles = jnp.stack(outs)[position ^ jnp.arange(size)]
+    incoming = joined_along(tiles, 0)
     panels = incoming[receive_index]
     attn = attend(lax.all_gather(panels, "member", axis=1, tiled=True), queries, live, scale)
     attn = attn.reshape(cand_rows, per_group, width)

time: 618 us -> 634 us (1.026)
  local copies, waits for them, and re-layouts: 143 us -> 164 us
  waiting for transfers between devices: 409 us -> 395 us
  starting transfers between devices: 5.96 us -> 13.4 us
    all_to_all x1 -> x0, waiting for transfers between devices: 47.4 us -> none  [on_device(): lax.all_to_all(outgoing, 'group', split_axis=0, concat_axis=0, tiled=True)]
    ppermute x0 -> x7, waiting for transfers between devices: none -> 31.5 us  [on_device(): lax.ppermute(sent, 'group', [(i, i ^ step) for i in range(size)])]
    ppermute x0 -> x7, starting transfers between devices: none -> 13.4 us  [on_device(): lax.ppermute(sent, 'group', [(i, i ^ step) for i in range(size)])]
    unnamed x10 -> x17, local copies, waits for them, and re-layouts: 1.98 us -> 14.2 us
  transfers between devices with their start and end apart: 2 -> 8, of which waited for: 2 -> 6; matrix products, arithmetic and copies ran while one was open for 1% -> 3% of each run, Pallas kernels for 0% -> 0%
where the time goes in v1:
time: 634 us; the launch traced here: 631 us
  waiting for transfers between devices  395 us (62%)
  local copies, waits for them, and re-layouts  164 us (26%)
  matrix products  36.4 us (6%)
  between operations  13.6 us (2%)
  starting transfers between devices  13.4 us (2%)
  other arithmetic  8.11 us (1%)
    all_gather x1, waiting for transfers between devices, on_device(): lax.all_gather(panels, 'member', axis=1, tiled=True)  363 us
    slice x2, local copies, waits for them, and re-layouts, attend(): piece[:, :, :width]  85.6 us
    slice x1, local copies, waits for them, and re-layouts, attend(): piece[:, :, width:]  42.2 us
    ppermute x7, waiting for transfers between devices, on_device(): lax.ppermute(sent, 'group', [(i, i ^ step) for i in range(size)])  31.5 us
    dot_general x1, matrix products, attend(): jnp.einsum('rhce,rehd->crhd', weights, values, preferred_element_type=jnp...  29.2 us
    unnamed x17, local copies, waits for them, and re-layouts  14.2 us
    ppermute x7, starting transfers between devices, on_device(): lax.ppermute(sent, 'group', [(i, i ^ step) for i in range(size)])  13.4 us
  transfers between devices with their start and end apart: 8, of which 6 were waited for; matrix products, arithmetic and copies ran while one was open for 3% of the time, Pallas kernels for 0%

profile of v1, /device:TPU:1, one launch (start us, length us, event | category | flops | bytes accessed | tf_op | source)
XLA Modules:
  0.0 630.8 jit_solution(1438096264367936419)
XLA Ops:
  8.2 5.0 gather_fusion
  13.2 4.5 broadcast_select_fusion
  17.7 3.6 constant_dynamic-slice_fusion.6
  24.3 3.0 collective-permute-start.3
  31.5 2.9 collective-permute-start.5
  34.5 1.9 bitcast_dynamic-update-slice_fusion.6
  36.4 4.1 collective-permute-start.6
  40.5 1.9 bitcast_dynamic-update-slice_fusion.5
  42.4 6.1 collective-permute-done.2
  48.5 1.9 bitcast_dynamic-update-slice_fusion.4
  50.4 11.1 %collective-permute-done.3 = bf16[1,128,2048]{2,1,0:T(8,128)(2,1)} collective-permute-done((bf16[1,128,2048]{2,1,0:T(8,128)(2,1)}, bf16[1,128,2048]{2,1,0:T(8,128)(2,1)}, u32[]{:S(2)}, u32[]{:S(2)}) %collective-permute-start.3) | collective-permute-done | bytes 524320 | tf_op jit(solution)/shard_map/ppermute | solution.py:92
  61.5 1.9 bitcast_dynamic-update-slice_fusion.3
  63.4 9.6 %collective-permute-done.4 = bf16[1,128,2048]{2,1,0:T(8,128)(2,1)} collective-permute-done((bf16[1,128,2048]{2,1,0:T(8,128)(2,1)}, bf16[1,128,2048]{2,1,0:T(8,128)(2,1)}, u32[]{:S(2)}, u32[]{:S(2)}) %collective-permute-start.4) | collective-permute-done | bytes 524320 | tf_op jit(solution)/shard_map/ppermute | solution.py:92
  73.0 1.9 bitcast_dynamic-update-slice_fusion.2
  75.7 4.7 collective-permute-done.6
  81.2 5.0 gather_fusion.1
  86.2 5.0 gather_fusion.4
  92.9 3.7 divide_multiply_fusion
  98.1 363.4 %all-gather.3.cloned.1.call-done = bf16[8,2048,2048]{2,1,0:T(8,128)(2,1)} async-done(((bf16[8,128,2048]{2,1,0:T(8,128)(2,1)}), bf16[8,2048,2048]{2,1,0:T(8,128)(2,1)}) %all-gather.3.cloned.1.call-update) | async-done | bytes 67108880 | tf_op jit(solution)/shard_map/all_gather | solution.py:96
  461.5 43.3 %fusion.38 = (bf16[8,2048,1024]{2,1,0:T(8,128)(2,1)}, bf16[8,2048,1024]{2,1,0:T(8,128)(2,1)}) fusion(bf16[8,2048,2048]{2,1,0:T(8,128)(2,1)} %all-gather.3.cloned.1.call-done), kind=kLoop, calls=%fused_computation.105 | loop fusion | bytes 134217728 | tf_op jit(solution)/shard_map/slice | solution.py:46
  504.8 42.2 %copy.43 = bf16[8,2048,1024]{1,2,0:T(8,128)(2,1)} copy(bf16[8,2048,1024]{2,1,0:T(8,128)(2,1)} %get-tuple-element.8) | data formatting | bytes 67108864 | tf_op jit(solution)/shard_map/slice | solution.py:47
  547.1 42.2 %copy.44 = bf16[8,2048,1024]{1,2,0:T(8,128)(2,1)} copy(bf16[8,2048,1024]{2,1,0:T(8,128)(2,1)} %get-tuple-element.7) | data formatting | bytes 67108864 | tf_op jit(solution)/shard_map/slice | solution.py:46
  589.3 29.2 %fusion.39 = (f32[32,8]{0,1:T(8,128)S(1)}, f32[32,8,8,128]{3,0,2,1:T(8,128)}) fusion(bf16[8,2048,8,128]{1,3,2,0:T(8,128)(2,1)} %bitcast.76, f32[8,2048]{1,0:T(8,128)S(1)} %convert_divide_fusion, bf16[8,2048,8,128]{1,3,2,0:T(8,128)(2,1)} %bitcast.77, bf16[32,8,8,128]{3,1,2,0:T(8,128)(2,1)S(1)} %fusion.12), kind=kOutput, calls=%fused_computation.106 | convolution fusion | flops 2177105664 | bytes 68748288 | tf_op jit(solution)/shard_map/rhce,rehd->crhd/dot_general | solution.py:52
  620.4 3.5 fusion.7
  (60 shorter events, 15.7 us)
Async XLA Ops:
  6.5 613.9 %copy-start = (bf16[1024,1024]{1,0:T(8,128)(2,1)S(1)}, bf16[1024,1024]{1,0:T(8,128)(2,1)}, u32[]{:S(2)}) copy-start(bf16[1024,1024]{1,0:T(8,128)(2,1)} %param.13) | copy-start | bytes 6291460
  6.5 455.0 %all-gather.3.cloned.1.call-start = ((), (), s32[]{:S(2)}) async-start(), calls=%async_computation | async-start | bytes 71303168 | tf_op jit(solution)/shard_map/all_gather | solution.py:96
  17.7 10.0 %copy-start.1 = (s32[64]{0:T(128)S(1)}, s32[64]{0:T(128)}, u32[]{:S(2)}) copy-start(s32[64]{0:T(128)} %param.10) | copy-start | bytes 772
  21.2 10.3 %collective-permute-start = (bf16[1,128,2048]{2,1,0:T(8,128)(2,1)}, bf16[1,128,2048]{2,1,0:T(8,128)(2,1)}, u32[]{:S(2)}, u32[]{:S(2)}) collective-permute-start(bf16[1,128,2048]{2,1,0:T(8,128)(2,1)} %get-tuple-element.15), channel_id=1, source_target_pairs={{0,16},{16,0},{32,48},{48,32},{64,80},{80,64},{96,112},{112,96},{1... | collective-permute-start | bytes 1572872 | tf_op jit(solution)/shard_map/ppermute | solution.py:92
  22.6 13.8 %collective-permute-start.1 = (bf16[1,128,2048]{2,1,0:T(8,128)(2,1)}, bf16[1,128,2048]{2,1,0:T(8,128)(2,1)}, u32[]{:S(2)}, u32[]{:S(2)}) collective-permute-start(bf16[1,128,2048]{2,1,0:T(8,128)(2,1)} %get-tuple-element.14), channel_id=1, source_target_pairs={{0,32},{16,48},{32,0},{48,16},{64,96},{80,112},{96,64},{112,80},{1... | collective-permute-start | bytes 1572872 | tf_op jit(solution)/shard_map/ppermute | solution.py:92
  24.0 24.4 %collective-permute-start.2 = (bf16[1,128,2048]{2,1,0:T(8,128)(2,1)}, bf16[1,128,2048]{2,1,0:T(8,128)(2,1)}, u32[]{:S(2)}, u32[]{:S(2)}) collective-permute-start(bf16[1,128,2048]{2,1,0:T(8,128)(2,1)} %get-tuple-element.13), channel_id=1, source_target_pairs={{0,48},{16,32},{32,16},{48,0},{64,112},{80,96},{96,80},{112,64},{1... | collective-permute-start | bytes 1572872 | tf_op jit(solution)/shard_map/ppermute | solution.py:92
  24.3 37.2 %collective-permute-start.3 = (bf16[1,128,2048]{2,1,0:T(8,128)(2,1)}, bf16[1,128,2048]{2,1,0:T(8,128)(2,1)}, u32[]{:S(2)}, u32[]{:S(2)}) collective-permute-start(bf16[1,128,2048]{2,1,0:T(8,128)(2,1)} %get-tuple-element.12), channel_id=1, source_target_pairs={{0,64},{16,80},{32,96},{48,112},{64,0},{80,16},{96,32},{112,48},{1... | collective-permute-start | bytes 1572872 | tf_op jit(solution)/shard_map/ppermute | solution.py:92
  27.3 45.7 %collective-permute-start.4 = (bf16[1,128,2048]{2,1,0:T(8,128)(2,1)}, bf16[1,128,2048]{2,1,0:T(8,128)(2,1)}, u32[]{:S(2)}, u32[]{:S(2)}) collective-permute-start(bf16[1,128,2048]{2,1,0:T(8,128)(2,1)} %get-tuple-element.11), channel_id=1, source_target_pairs={{0,80},{16,64},{32,112},{48,96},{64,16},{80,0},{96,48},{112,32},{1... | collective-permute-start | bytes 1572872 | tf_op jit(solution)/shard_map/ppermute | solution.py:92
  31.5 43.3 %collective-permute-start.5 = (bf16[1,128,2048]{2,1,0:T(8,128)(2,1)S(1)}, bf16[1,128,2048]{2,1,0:T(8,128)(2,1)S(1)}, u32[]{:S(2)}, u32[]{:S(2)}) collective-permute-start(bf16[1,128,2048]{2,1,0:T(8,128)(2,1)S(1)} %get-tuple-element.10), channel_id=1, source_target_pairs={{0,96},{16,112},{32,64},{48,80},{64,32},{80,48},{96,0},{112,16},{1... | collective-permute-start | bytes 1572872 | tf_op jit(solution)/shard_map/ppermute | solution.py:92
  36.4 43.9 %collective-permute-start.6 = (bf16[1,128,2048]{2,1,0:T(8,128)(2,1)S(1)}, bf16[1,128,2048]{2,1,0:T(8,128)(2,1)S(1)}, u32[]{:S(2)}, u32[]{:S(2)}) collective-permute-start(bf16[1,128,2048]{2,1,0:T(8,128)(2,1)S(1)} %get-tuple-element.9), channel_id=1, source_target_pairs={{0,112},{16,96},{32,80},{48,64},{64,48},{80,32},{96,16},{112,0},{1... | collective-permute-start | bytes 1572872 | tf_op jit(solution)/shard_map/ppermute | solution.py:92
  91.2 0.7 copy-start.2
  91.2 1.3 copy-start.3
  96.6 1.4 copy-start.4
Sparse Core Ops, SparseCore 0:
  91.3 370.1 all-gather.2
